TPU v7x, 32 devices: a whole 2x2x4 slice. The times are simulated.
32 devices in a mesh: amp: 8 (over y, x, core), int: 4 (over z).
Axes of the slice: x: 2, y: 2, z: 4, core: 2. Of those that a mesh axis runs over, the one named last changes fastest.
Arguments:
- amplitudes: float32 [768, 512], P('int'), may hold values from -6 to 6
- slab_integrals: float32 [512, 51200], P('int', 'amp'), may hold values from -0.25 to 0.25
- cycle_integrals: float32 [96, 800, 512], P('int', 'amp'), may hold values from -0.03125 to 0.03125
- occ_irrep: int32 [96], replicated, may hold values from 0 to 7
- vir_irrep: int32 [800], replicated, may hold values from 0 to 7
Outputs:
- ladder: float32 [768, 51200], P('int', 'amp')
- cycle: float32 [512, 512], P('int', 'amp')
All inputs are finite; a program needn't handle non-finite values.
Results may differ from a plain program's by a relative error of at most 0.00011.
Values sent between devices are 32-bit elements; how exact they have to be, the bound alone decides.
No kernel may reach another device: no remote copies, remote signals or barrier semaphores. Data moves between devices by JAX's collectives and lax.ppermute only.
A program may use at most 64 MiB of HBM per device.

v0:
```python
import jax
import jax.numpy as jnp
from jax import lax
from jax.sharding import PartitionSpec as P

PRECISION = lax.Precision.HIGH


def per_device(amplitudes, slab_integrals, cycle_integrals, occ_irrep, vir_irrep, n_amp, n_int):
    nocc = occ_irrep.shape[0]
    nvir = vir_irrep.shape[0]
    rows, pw = amplitudes.shape
    pw_local = slab_integrals.shape[0]
    i_local = rows // nocc
    ibat = i_local * n_int
    width = slab_integrals.shape[1]
    a_local = width // nvir
    slab = a_local * n_amp
    k_local, c_local, columns = cycle_integrals.shape
    if a_local >= 4:
        sizes = [(a_local - 1) // 2, a_local - 2 - (a_local - 1) // 2, 1, 1]
    elif a_local >= 2:
        sizes = [a_local - 1, 1]
    else:
        sizes = [a_local]
    chunks = len(sizes)
    starts = [sum(sizes[:t]) for t in range(chunks)]
    t_cyc = lax.all_to_all(
        amplitudes.reshape(i_local, nocc, pw), "int", split_axis=1, concat_axis=0, tiled=True
    ).reshape(ibat * k_local, pw)
    w2 = cycle_integrals.transpose(1, 0, 2).reshape(c_local * k_local, columns)
    ladder_chunks = []
    cycle_chunks = []
    for t in range(chunks):
        a_chunk = sizes[t]
        v = lax.slice_in_dim(slab_integrals, starts[t] * nvir, (starts[t] + a_chunk) * nvir, axis=1)
        v_all = lax.all_gather(v, "int", axis=0, tiled=True)
        if t:
            v_all, ladder_chunks[-1], cycle_chunks[-1] = lax.optimization_barrier(
                (v_all, ladder_chunks[-1], cycle_chunks[-1])
            )
        ladder_chunks.append(
            jnp.dot(amplitudes, v_all, precision=PRECISION, preferred_element_type=jnp.float32)
        )
        l_cyc = jnp.dot(t_cyc, v_all, precision=PRECISION, preferred_element_type=jnp.float32)
        l_cyc = l_cyc.reshape(ibat, k_local, a_chunk, n_amp, c_local).transpose(3, 0, 2, 4, 1)
        l_cyc = l_cyc.reshape(n_amp, ibat * a_chunk, c_local * k_local)
        moved = lax.all_to_all(l_cyc, "amp", split_axis=0, concat_axis=0, tiled=True)
        moved = moved.reshape(n_amp * ibat * a_chunk, c_local * k_local)
        cycle_chunks.append(
            jnp.dot(moved, w2, precision=PRECISION, preferred_element_type=jnp.float32)
        )
    ladder = jnp.concatenate(ladder_chunks, axis=1)
    parts = jnp.concatenate(
        [c.reshape(n_amp, ibat, sizes[t], columns) for t, c in enumerate(cycle_chunks)], axis=2
    )
    col_local = columns // n_amp
    parts = parts.transpose(1, 0, 2, 3).reshape(n_int, i_local * slab, n_amp, col_local)
    parts = parts.transpose(0, 2, 1, 3).reshape(n_int * n_amp, i_local * slab, col_local)
    gathered = lax.all_to_all(parts, ("int", "amp"), split_axis=0, concat_axis=0, tiled=True)
    sums = jnp.sum(gathered, axis=0)
    row_start = lax.axis_index("int") * i_local
    batch_labels = lax.dynamic_slice_in_dim(occ_irrep, row_start, i_local, 0)
    slab_labels = vir_irrep[:slab]
    row_labels = jnp.bitwise_xor(batch_labels[:, None], slab_labels[None, :]).reshape(-1)
    col_ids = lax.axis_index("amp") * col_local + jnp.arange(col_local, dtype=jnp.int32)
    col_occ = col_ids // slab
    col_vir = col_ids % slab
    occ_match = col_occ[:, None] == jnp.arange(nocc, dtype=jnp.int32)[None, :]
    vir_match = col_vir[:, None] == jnp.arange(slab, dtype=jnp.int32)[None, :]
    occ_lookup = jnp.sum(jnp.where(occ_match, occ_irrep[None, :], 0), axis=1)
    vir_lookup = jnp.sum(jnp.where(vir_match, slab_labels[None, :], 0), axis=1)
    col_labels = jnp.bitwise_xor(occ_lookup, vir_lookup)
    keep = row_labels[:, None] == col_labels[None, :]
    cycle = jnp.where(keep, sums, jnp.zeros_like(sums))
    return (ladder, cycle)


def solution(mesh):
    n_amp = mesh.shape["amp"]
    n_int = mesh.shape["int"]
    in_specs = (P("int", None), P("int", "amp"), P("int", "amp", None), P(), P())
    out_specs = (P("int", "amp"), P("int", "amp"))

    def body(*args):
        return per_device(*args, n_amp=n_amp, n_int=n_int)

    return jax.shard_map(body, mesh=mesh, in_specs=in_specs, out_specs=out_specs, check_vma=False)
```

profile of v0, /device:TPU:0, one launch (start us, length us, event | category | flops | bytes accessed | tf_op | source)
XLA Modules:
  0.0 353.6 jit_solution(3028213121475945152)
XLA Ops:
  12.1 27.5 %all_to_all.40 = f32[2,96,512]{2,0,1:T(2,128)S(1)} all-to-all(f32[2,96,512]{2,0,1:T(2,128)S(1)} %copy.57), channel_id=1, replica_groups=mesh['amp'=8,'int'=4] {'int'}, dimensions={1} | all-to-all | bytes 786432 | tf_op jit(solution)/shard_map/all_to_all | solution.py:28
  39.7 71.0 %all-gather.7.cloned.1.call-done = f32[512,2400]{1,0:T(8,128)} async-done(((f32[128,2400]{1,0:T(8,128)}), f32[512,2400]{1,0:T(8,128)}) %all-gather.7.cloned.1.call-update) | async-done | bytes 4915216 | tf_op jit(solution)/shard_map/all_gather | solution.py:37
  110.7 5.7 %copy.60 = f32[2400,512]{1,0:T(8,128)} copy(f32[2400,512]{0,1:T(8,128)} %bitcast.79) | data formatting | bytes 9830400 | tf_op jit(solution)/shard_map/dot_general | solution.py:45
  116.4 5.4 %reshape.144 = f32[3,8,100,512,1]{3,2,1,0,4:T(8,128)} reshape(f32[2400,512]{1,0:T(8,128)} %copy.60) | data formatting | bytes 9830400 | tf_op jit(solution)/shard_map/dot_general | solution.py:45
  121.9 4.9 %convolution_bitcast_fusion.2 = f32[8,8,3,100,24]{3,4,0,2,1:T(8,128)S(1)} fusion(f32[8,24,512,1,1]{2,1,4,3,0:T(8,128)S(1)} %bitcast.82, f32[3,8,100,512,1]{3,2,1,0,4:T(8,128)} %reshape.144), kind=kOutput, calls=%fused_computation.2 | convolution fusion | flops 1415577600 | bytes 7151616 | tf_op jit(solution)/shard_map/dot_general | solution.py:45
  126.8 5.6 %copy.61 = f32[8,8,3,100,24]{4,3,2,1,0:T(8,128)} copy(f32[8,8,3,100,24]{3,4,0,2,1:T(8,128)S(1)} %convolution_bitcast_fusion.2) | data formatting | bytes 3686400 | tf_op jit(solution)/shard_map/transpose | solution.py:46
  132.5 7.6 %reshape.126 = f32[8,24,2400]{2,1,0:T(8,128)} reshape(f32[8,8,3,100,24]{4,3,2,1,0:T(8,128)} %copy.61) | data formatting | bytes 3686400 | tf_op jit(solution)/shard_map/reshape | solution.py:47
  146.6 5.6 %fusion.4 = f32[192,2400]{1,0:T(8,128)} fusion(f32[192,512]{1,0:T(8,128)S(1)} %copy-done.2, f32[512,2400]{1,0:T(8,128)} %all-gather.7.cloned.1.call-done), kind=kOutput, calls=%fused_computation.25 | convolution fusion | flops 1415577600 | bytes 7151616 | tf_op jit(solution)/shard_map/dot_general | solution.py:43
  152.2 15.8 %all-to-all-done.1 = f32[8,24,2400]{2,1,0:T(8,128)S(1)} async-done(((f32[8,24,2400]{2,1,0:T(8,128)}), f32[8,24,2400]{2,1,0:T(8,128)S(1)}, u32[]{:S(2)}, u32[]{:S(2)}) %all-to-all-start.1) | async-done | bytes 1843232 | tf_op jit(solution)/shard_map/all_to_all | solution.py:48
  168.0 5.1 %fusion.5 = f32[192,512]{1,0:T(8,128)} fusion(f32[192,2400]{1,0:T(8,128)S(1)} %bitcast.88, f32[2400,512]{1,0:T(8,128)} %bitcast.74), kind=kOutput, calls=%fused_computation.26 | convolution fusion | flops 1415577600 | bytes 7151616 | tf_op jit(solution)/shard_map/dot_general | solution.py:51
  173.2 32.0 %all-gather.5.cloned.1.call-done = f32[512,2400]{1,0:T(8,128)} async-done(((f32[128,2400]{1,0:T(8,128)}), f32[512,2400]{1,0:T(8,128)}) %all-gather.5.cloned.1.call-update) | async-done | bytes 4915216 | tf_op jit(solution)/shard_map/all_gather | solution.py:37
  205.2 5.5 %convolution_bitcast_fusion = f32[192,2400]{1,0:T(8,128)} fusion(f32[512,2400]{1,0:T(8,128)} %all-gather.5.cloned.1.call-done, f32[192,512]{1,0:T(8,128)S(1)} %bitcast.83), kind=kOutput, calls=%fused_computation | convolution fusion | flops 1415577600 | bytes 7151616 | tf_op jit(solution)/shard_map/dot_general | solution.py:45
  213.3 5.6 %copy.63 = f32[8,24,3,8,100]{1,4,2,0,3:T(8,128)} copy(f32[8,24,3,8,100]{4,3,2,1,0:T(8,128)S(1)} %reshape.130) | data formatting | bytes 3686400 | tf_op jit(solution)/shard_map/reshape | solution.py:46
  218.9 7.6 %reshape.131 = f32[8,24,2400]{2,1,0:T(8,128)} reshape(f32[8,8,3,100,24]{4,3,2,1,0:T(8,128)} %bitcast.78) | data formatting | bytes 3686400 | tf_op jit(solution)/shard_map/reshape | solution.py:47
  230.6 5.5 %convolution_bitcast_fusion.1 = f32[192,2400]{1,0:T(8,128)} fusion(f32[512,2400]{1,0:T(8,128)} %all-gather.5.cloned.1.call-done, f32[192,512]{1,0:T(8,128)S(1)} %copy-done.2), kind=kOutput, calls=%fused_computation.1 | convolution fusion | flops 1415577600 | bytes 7151616 | tf_op jit(solution)/shard_map/dot_general | solution.py:43
  236.1 18.1 %all-to-all-done.2 = f32[8,24,2400]{2,1,0:T(8,128)S(1)} async-done(((f32[8,24,2400]{2,1,0:T(8,128)}), f32[8,24,2400]{2,1,0:T(8,128)S(1)}, u32[]{:S(2)}, u32[]{:S(2)}) %all-to-all-start.2) | async-done | bytes 1843232 | tf_op jit(solution)/shard_map/all_to_all | solution.py:48
  254.3 5.2 %fusion.6 = f32[192,512]{1,0:T(8,128)} fusion(f32[192,2400]{1,0:T(8,128)S(1)} %bitcast.89, f32[2400,512]{1,0:T(8,128)} %bitcast.75), kind=kOutput, calls=%fused_computation.27 | convolution fusion | flops 1415577600 | bytes 7151616 | tf_op jit(solution)/shard_map/dot_general | solution.py:51
  273.8 7.5 %all-to-all-done.3 = f32[8,8,2400]{2,1,0:T(8,128)S(1)} async-done(((f32[8,8,2400]{2,1,0:T(8,128)}), f32[8,8,2400]{2,1,0:T(8,128)S(1)}, u32[]{:S(2)}, u32[]{:S(2)}) %all-to-all-start.3) | async-done | bytes 614432 | tf_op jit(solution)/shard_map/all_to_all | solution.py:48
  281.3 4.0 %fusion = f32[64,512]{1,0:T(8,128)S(1)} fusion(f32[2400,512]{1,0:T(8,128)} %bitcast.76, f32[8,8,2400]{2,1,0:T(8,128)S(1)} %all-to-all-done.3), kind=kOutput, calls=%fused_computation.9 | convolution fusion | flops 471859200 | bytes 5660672 | tf_op jit(solution)/shard_map/dot_general | solution.py:51
  295.9 3.9 %all-to-all-start.4 = ((f32[8,8,2400]{2,1,0:T(8,128)}), f32[8,8,2400]{2,1,0:T(8,128)S(1)}, u32[]{:S(2)}, u32[]{:S(2)}) async-start(f32[8,8,2400]{2,1,0:T(8,128)} %reshape.140), calls=%async_computation.4 | async-start | bytes 1245184 | tf_op jit(solution)/shard_map/all_to_all | solution.py:48
  301.3 9.2 %all-to-all-done.4 = f32[8,8,2400]{2,1,0:T(8,128)S(1)} async-done(((f32[8,8,2400]{2,1,0:T(8,128)}), f32[8,8,2400]{2,1,0:T(8,128)S(1)}, u32[]{:S(2)}, u32[]{:S(2)}) %all-to-all-start.4) | async-done | bytes 614432 | tf_op jit(solution)/shard_map/all_to_all | solution.py:48
  310.5 4.0 %convolution_bitcast_fusion.7 = f32[8,8,1,512]{3,1,0,2:T(8,128)S(1)} fusion(f32[8,8,2400]{2,1,0:T(8,128)S(1)} %all-to-all-done.4, f32[2400,512,1]{1,0,2:T(8,128)} %bitcast.77), kind=kOutput, calls=%fused_computation.7 | convolution fusion | flops 471859200 | bytes 5660672 | tf_op jit(solution)/shard_map/dot_general | solution.py:51
  324.6 6.0 %concatenate.6 = f32[192,6400]{1,0:T(8,128)} concatenate(f32[192,2400]{1,0:T(8,128)S(1)} %copy-done.4, f32[192,2400]{1,0:T(8,128)} %convolution_bitcast_fusion.1, f32[192,800]{1,0:T(8,128)} %convolution_bitcast_fusion.6, f32[192,800]{1,0:T(8,128)} %convolution_bitcast_fusion.4), dimensions={1} | concatenate | bytes 9830400 | tf_op jit(solution)/shard_map/concatenate | solution.py:53
  330.6 15.7 %all-to-all-done.5 = f32[32,128,64]{1,2,0:T(8,128)S(1)} async-done(((f32[32,128,64]{1,2,0:T(8,128)}), f32[32,128,64]{1,2,0:T(8,128)S(1)}, u32[]{:S(2)}, u32[]{:S(2)}) %all-to-all-start.5) | async-done | bytes 1048608 | tf_op jit(solution)/shard_map/all_to_all | solution.py:60
  (62 shorter events, 55.4 us)
Async XLA Ops:
  7.2 103.6 %all-gather.7.cloned.1.call-start = ((), (), s32[]{:S(2)}) async-start(), calls=%async_computation.7 | async-start | bytes 6225920 | tf_op jit(solution)/shard_map/all_gather | solution.py:37
  10.8 1.0 copy-start.2
  10.8 194.3 %all-gather.5.cloned.1.call-start = ((), (), s32[]{:S(2)}) async-start(), calls=%async_computation.6 | async-start | bytes 6225920 | tf_op jit(solution)/shard_map/all_gather | solution.py:37
  39.7 219.8 %copy-start = (f32[4,2,24,512]{3,2,1,0:T(8,128)}, f32[4,2,24,512]{3,2,1,0:T(8,128)S(1)}, u32[]{:S(2)}) copy-start(f32[4,2,24,512]{3,2,1,0:T(8,128)S(1)} %copy.59) | copy-start | bytes 1179652
  140.1 28.0 %all-to-all-start.1 = ((f32[8,24,2400]{2,1,0:T(8,128)}), f32[8,24,2400]{2,1,0:T(8,128)S(1)}, u32[]{:S(2)}, u32[]{:S(2)}) async-start(f32[8,24,2400]{2,1,0:T(8,128)} %reshape.126), calls=%async_computation.1 | async-start | bytes 3735552 | tf_op jit(solution)/shard_map/all_to_all | solution.py:48
  143.9 115.6 %all-gather.9.cloned.1.call-start = ((), (), s32[]{:S(2)}) async-start(), calls=%async_computation.8 | async-start | bytes 2293760 | tf_op jit(solution)/shard_map/all_gather | solution.py:37
  226.5 27.8 %all-to-all-start.2 = ((f32[8,24,2400]{2,1,0:T(8,128)}), f32[8,24,2400]{2,1,0:T(8,128)S(1)}, u32[]{:S(2)}, u32[]{:S(2)}) async-start(f32[8,24,2400]{2,1,0:T(8,128)} %reshape.131), calls=%async_computation.2 | async-start | bytes 3735552 | tf_op jit(solution)/shard_map/all_to_all | solution.py:48
  230.1 58.3 %all-gather.11.cloned.1.call-start = ((), (), s32[]{:S(2)}) async-start(), calls=%async_computation.9 | async-start | bytes 2293760 | tf_op jit(solution)/shard_map/all_gather | solution.py:37
  267.1 14.3 %all-to-all-start.3 = ((f32[8,8,2400]{2,1,0:T(8,128)}), f32[8,8,2400]{2,1,0:T(8,128)S(1)}, u32[]{:S(2)}, u32[]{:S(2)}) async-start(f32[8,8,2400]{2,1,0:T(8,128)} %reshape.134), calls=%async_computation.3 | async-start | bytes 1245184 | tf_op jit(solution)/shard_map/all_to_all | solution.py:48
  273.8 14.5 %copy-start.1 = (f32[4,2,24,512]{3,2,1,0:T(8,128)S(1)}, f32[4,2,24,512]{3,2,1,0:T(8,128)}, u32[]{:S(2)}) copy-start(f32[4,2,24,512]{3,2,1,0:T(8,128)} %copy-done) | copy-start | bytes 1179652
  295.9 5.1 %copy-start.5 = (f32[192,512]{1,0:T(8,128)S(1)}, f32[192,512]{1,0:T(8,128)}, u32[]{:S(2)}) copy-start(f32[192,512]{1,0:T(8,128)} %fusion.6) | copy-start | bytes 1179652
  295.9 14.6 %all-to-all-start.4 = ((f32[8,8,2400]{2,1,0:T(8,128)}), f32[8,8,2400]{2,1,0:T(8,128)S(1)}, u32[]{:S(2)}, u32[]{:S(2)}) async-start(f32[8,8,2400]{2,1,0:T(8,128)} %reshape.140), calls=%async_computation.4 | async-start | bytes 1245184 | tf_op jit(solution)/shard_map/all_to_all | solution.py:48
  315.7 5.1 %copy-start.6 = (s32[96]{0:T(128)S(1)}, s32[96]{0:T(128)}, u32[]{:S(2)}) copy-start(s32[96]{0:T(128)} %param.8) | copy-start | bytes 1156
  315.7 5.7 %copy-start.3 = (f32[192,512]{1,0:T(8,128)S(1)}, f32[192,512]{1,0:T(8,128)}, u32[]{:S(2)}) copy-start(f32[192,512]{1,0:T(8,128)} %param.5) | copy-start | bytes 1179652
  317.3 7.3 %copy-start.4 = (f32[192,2400]{1,0:T(8,128)S(1)}, f32[192,2400]{1,0:T(8,128)}, u32[]{:S(2)}) copy-start(f32[192,2400]{1,0:T(8,128)} %fusion.4) | copy-start | bytes 5529604
  317.3 29.0 %all-to-all-start.5 = ((f32[32,128,64]{1,2,0:T(8,128)}), f32[32,128,64]{1,2,0:T(8,128)S(1)}, u32[]{:S(2)}, u32[]{:S(2)}) async-start(f32[32,128,64]{1,2,0:T(8,128)} %bitcast.30), calls=%async_computation.5 | async-start | bytes 2097152 | tf_op jit(solution)/shard_map/all_to_all | solution.py:60
Sparse Core Ops, SparseCore 0:
  11.0 99.7 all-gather.6
  112.3 92.8 all-gather.4
  206.8 39.7 all-gather.8
  248.0 40.2 all-gather.10
where the time goes:
time: 355 us; the launch traced here: 354 us
  waiting for transfers between devices  173 us (49%)
  local copies, waits for them, and re-layouts  68 us (19%)
  matrix products  50.8 us (14%)
  blocking collectives  27.5 us (8%)
  starting transfers between devices  18.2 us (5%)
  between operations  14 us (4%)
    all_gather x4, waiting for transfers between devices, per_device(): v_all = lax.all_gather(v, 'int', axis=0, tiled=True)  106 us
    all_to_all x4, waiting for transfers between devices, per_device(): lax.all_to_all(l_cyc, 'amp', split_axis=0, concat_axis=0, tiled=True)  50.6 us
    all_to_all x1, blocking collectives, per_device(): lax.all_to_all(amplitudes.reshape(i_local, nocc, pw), 'int', split_axis=1...  27.5 us
    reshape x4, local copies, waits for them, and re-layouts, per_device(): l_cyc = l_cyc.reshape(n_amp, ibat * a_chunk, c_local * k_local)  18.7 us
    dot_general x4, matrix products, per_device(): jnp.dot(moved, w2, precision=PRECISION, preferred_element_type=jnp.float32)  18.4 us
    dot_general x4, matrix products, per_device(): jnp.dot(amplitudes, v_all, precision=PRECISION, preferred_element_type=jn...  17.4 us
    all_to_all x1, waiting for transfers between devices, per_device(): lax.all_to_all(parts, ('int', 'amp'), split_axis=0, concat_axis=0, tiled=...  15.7 us
    reshape x6, local copies, waits for them, and re-layouts, per_device(): l_cyc.reshape(ibat, k_local, a_chunk, n_amp, c_local)  15.3 us
  transfers between devices with their start and end apart: 9, of which 8 were waited for; matrix products, arithmetic and copies ran while one was open for 29% of the time, Pallas kernels for 0%

commit v1 on v0

--- a/solution.py
+++ b/solution.py
@@ -34,7 +34,15 @@
     for t in range(chunks):
         a_chunk = sizes[t]
         v = lax.slice_in_dim(slab_integrals, starts[t] * nvir, (starts[t] + a_chunk) * nvir, axis=1)
-        v_all = lax.all_gather(v, "int", axis=0, tiled=True)
+        ways, here, step = (lax.axis_size("int"), lax.axis_index("int"), v.shape[0])
+        line, have = (v, 1)
+        while have < ways:
+            line = jnp.concatenate(
+                [line, lax.ppermute(line, "int", [(d, (d - have) % ways) for d in range(ways)])],
+                axis=0,
+            )
+            have = 2 * have
+        v_all = jnp.roll(line, here * step, axis=0)
         if t:
             v_all, ladder_chunks[-1], cycle_chunks[-1] = lax.optimization_barrier(
                 (v_all, ladder_chunks[-1], cycle_chunks[-1])

time: 355 us -> 488 us (1.37); the launches traced: 354 us -> 480 us
  starting transfers between devices: 18.2 us -> 122 us
  waiting for transfers between devices: 173 us -> 215 us
  blocking collectives: 27.5 us -> 0 us
  other arithmetic: 1.68 us -> 21.5 us
  between operations: 14 us -> 1.2 us
  local copies, waits for them, and re-layouts: 68 us -> 74.9 us
  matrix products: 50.8 us -> 45.7 us
    ppermute x0 -> x8, waiting for transfers between devices: none -> 135 us  [per_device(): lax.ppermute(line, 'int', [(d, (d - have) % ways) for d in range(ways)])]
    all_gather x4 -> x0, waiting for transfers between devices: 106 us -> none  [per_device(): v_all = lax.all_gather(v, 'int', axis=0, tiled=True)]
    ppermute x0 -> x8, starting transfers between devices: none -> 98.4 us  [per_device(): lax.ppermute(line, 'int', [(d, (d - have) % ways) for d in range(ways)])]
    all_to_all x0 -> x1, waiting for transfers between devices: none -> 54.5 us  [per_device(): lax.all_to_all(amplitudes.reshape(i_local, nocc, pw), 'int', split_axis=1...]
    all_to_all x4, waiting for transfers between devices: 50.6 us -> 8.67 us  [per_device(): lax.all_to_all(l_cyc, 'amp', split_axis=0, concat_axis=0, tiled=True)]
    all_to_all x1 -> x0, blocking collectives: 27.5 us -> none  [per_device(): lax.all_to_all(amplitudes.reshape(i_local, nocc, pw), 'int', split_axis=1...]
    concatenate x0 -> x8, other arithmetic: none -> 19.8 us  [the longest x4 13.1 us: per_device(): v_all = jnp.roll(line, here * step, axis=0)]
    dot_general x2 -> x0, local copies, waits for them, and re-layouts: 11.1 us -> none  [per_device(): jnp.dot(t_cyc, v_all, precision=PRECISION, preferred_element_type=jnp.flo...]
  transfers between devices with their start and end apart: 9 -> 14, of which waited for: 8 -> 8; matrix products, arithmetic and copies ran while one was open for 29% -> 23% of each run, Pallas kernels for 0% -> 0%
where the time goes in v1:
time: 488 us; the launch traced here: 480 us
  waiting for transfers between devices  215 us (44%)
  starting transfers between devices  122 us (25%)
  local copies, waits for them, and re-layouts  74.9 us (15%)
  matrix products  45.7 us (9%)
  other arithmetic  21.5 us (4%)
    ppermute x8, waiting for transfers between devices, per_device(): lax.ppermute(line, 'int', [(d, (d - have) % ways) for d in range(ways)])  135 us
    ppermute x8, starting transfers between devices, per_device(): lax.ppermute(line, 'int', [(d, (d - have) % ways) for d in range(ways)])  98.4 us
    all_to_all x1, waiting for transfers between devices, per_device(): lax.all_to_all(amplitudes.reshape(i_local, nocc, pw), 'int', split_axis=1...  54.5 us
    reshape x8, local copies, waits for them, and re-layouts, per_device(): l_cyc.reshape(ibat, k_local, a_chunk, n_amp, c_local)  24.6 us
    reshape x4, local copies, waits for them, and re-layouts, per_device(): l_cyc = l_cyc.reshape(n_amp, ibat * a_chunk, c_local * k_local)  21.7 us
    dot_general x4, matrix products, per_device(): jnp.dot(moved, w2, precision=PRECISION, preferred_element_type=jnp.float32)  19.8 us
    all_to_all x4, starting transfers between devices, per_device(): lax.all_to_all(l_cyc, 'amp', split_axis=0, concat_axis=0, tiled=True)  16.8 us
    all_to_all x1, waiting for transfers between devices, per_device(): lax.all_to_all(parts, ('int', 'amp'), split_axis=0, concat_axis=0, tiled=...  16.4 us
  transfers between devices with their start and end apart: 14, of which 8 were waited for; matrix products, arithmetic and copies ran while one was open for 23% of the time, Pallas kernels for 0%

profile of v1, /device:TPU:0, one launch (start us, length us, event | category | flops | bytes accessed | tf_op | source)
XLA Modules:
  0.0 480.3 jit_solution(686426005291477948)
XLA Ops:
  5.8 5.1 %collective-permute-start.2 = (f32[128,2400]{0,1:T(8,128)S(1)}, f32[128,2400]{0,1:T(8,128)S(1)}, u32[]{:S(2)}, u32[]{:S(2)}) collective-permute-start(f32[128,2400]{0,1:T(8,128)S(1)} %copy.72), channel_id=1, source_target_pairs={{0,3},{1,0},{2,1},{3,2},{4,7},{5,4},{6,5},{7,6},{8,11},{9,8},{10,9... | collective-permute-start | bytes 3686408 | tf_op jit(solution)/shard_map/ppermute | solution.py:41
  10.9 26.3 %collective-permute-done.2 = f32[128,2400]{0,1:T(8,128)S(1)} collective-permute-done((f32[128,2400]{0,1:T(8,128)S(1)}, f32[128,2400]{0,1:T(8,128)S(1)}, u32[]{:S(2)}, u32[]{:S(2)}) %collective-permute-start.2) | collective-permute-done | bytes 1228832 | tf_op jit(solution)/shard_map/ppermute | solution.py:41
  49.7 71.3 %collective-permute-done = f32[128,2400]{0,1:T(8,128)} collective-permute-done((f32[128,2400]{0,1:T(8,128)S(1)}, f32[128,2400]{0,1:T(8,128)}, u32[]{:S(2)}, u32[]{:S(2)}) %collective-permute-start) | collective-permute-done | bytes 1228832 | tf_op jit(solution)/shard_map/ppermute | solution.py:41
  123.8 58.0 %collective-permute-start.1 = (f32[256,2400]{0,1:T(8,128)}, f32[256,2400]{0,1:T(8,128)}, u32[]{:S(2)}, u32[]{:S(2)}) collective-permute-start(f32[256,2400]{0,1:T(8,128)} %pad_maximum_fusion), channel_id=1, source_target_pairs={{0,2},{1,3},{2,0},{3,1},{4,6},{5,7},{6,4},{7,5},{8,10},{9,11},{10,... | collective-permute-start | bytes 7372808 | tf_op jit(solution)/shard_map/ppermute | solution.py:41
  181.9 54.5 %all-to-all-done = f32[2,96,512]{2,0,1:T(2,128)S(1)} async-done(((f32[2,96,512]{2,0,1:T(2,128)}), f32[2,96,512]{2,0,1:T(2,128)S(1)}, u32[]{:S(2)}, u32[]{:S(2)}) %all-to-all-start) | async-done | bytes 393248 | tf_op jit(solution)/shard_map/all_to_all | solution.py:28
  249.8 7.2 %copy.61 = f32[8,24,3,8,100]{1,4,2,0,3:T(8,128)} copy(f32[8,24,3,8,100]{4,3,2,1,0:T(8,128)} %reshape.126) | data formatting | bytes 3686400 | tf_op jit(solution)/shard_map/reshape | solution.py:54
  257.0 7.5 %reshape.127 = f32[8,24,2400]{2,1,0:T(8,128)} reshape(f32[8,8,3,100,24]{4,3,2,1,0:T(8,128)} %bitcast.75) | data formatting | bytes 3686400 | tf_op jit(solution)/shard_map/reshape | solution.py:55
  273.2 6.2 %convolution_bitcast_fusion.3 = f32[192,2400]{1,0:T(8,128)} fusion(f32[512,2400]{0,1:T(8,128)} %copy-done.1, f32[192,512]{1,0:T(8,128)S(1)} %copy-done.2), kind=kOutput, calls=%fused_computation.25 | convolution fusion | flops 1415577600 | bytes 7151616 | tf_op jit(solution)/shard_map/dot_general | solution.py:51
  279.3 9.9 %collective-permute-done.1 = f32[256,2400]{0,1:T(8,128)} collective-permute-done((f32[256,2400]{0,1:T(8,128)}, f32[256,2400]{0,1:T(8,128)}, u32[]{:S(2)}, u32[]{:S(2)}) %collective-permute-start.1) | collective-permute-done | bytes 2457632 | tf_op jit(solution)/shard_map/ppermute | solution.py:41
  289.2 5.2 %fusion.7 = f32[512,2400]{0,1:T(8,128)} fusion(s32[]{:T(128)S(6)} %select_n.62, f32[128,2400]{0,1:T(8,128)S(1)} %copy.71, f32[128,2400]{0,1:T(8,128)} %collective-permute-done, f32[256,2400]{0,1:T(8,128)} %collective-permute-done.1), kind=kLoop, calls=%fused_computation.19 | loop fusion | flops 6144000 | bytes 9830404 | tf_op jit(solution)/shard_map/jit(_roll_dynamic)/concatenate | solution.py:45
  294.4 5.8 %fusion.24 = f32[192,512]{1,0:T(8,128)} fusion(f32[192,2400]{1,0:T(8,128)} %bitcast.7, f32[2400,512]{1,0:T(8,128)} %bitcast.71), kind=kOutput, calls=%fused_computation.74 | convolution fusion | flops 1415577600 | bytes 7151616 | tf_op jit(solution)/shard_map/dot_general | solution.py:59
  306.6 5.6 %copy.63 = f32[8,24,3,8,100]{1,4,2,0,3:T(8,128)} copy(f32[8,24,3,8,100]{4,3,2,1,0:T(8,128)S(1)} %reshape.130) | data formatting | bytes 3686400 | tf_op jit(solution)/shard_map/reshape | solution.py:54
  312.1 7.6 %reshape.131 = f32[8,24,2400]{2,1,0:T(8,128)} reshape(f32[8,8,3,100,24]{4,3,2,1,0:T(8,128)} %bitcast.76) | data formatting | bytes 3686400 | tf_op jit(solution)/shard_map/reshape | solution.py:55
  319.7 4.5 all-to-all-start.2
  325.7 9.5 %collective-permute-start.6 = (f32[128,800]{0,1:T(8,128)S(1)}, f32[128,800]{0,1:T(8,128)S(1)}, u32[]{:S(2)}, u32[]{:S(2)}) collective-permute-start(f32[128,800]{0,1:T(8,128)S(1)} %copy.74), channel_id=1, source_target_pairs={{0,3},{1,0},{2,1},{3,2},{4,7},{5,4},{6,5},{7,6},{8,11},{9,8},{10,9... | collective-permute-start | bytes 1228808 | tf_op jit(solution)/shard_map/ppermute | solution.py:41
  335.2 17.4 %collective-permute-done.6 = f32[128,800]{0,1:T(8,128)S(1)} collective-permute-done((f32[128,800]{0,1:T(8,128)S(1)}, f32[128,800]{0,1:T(8,128)S(1)}, u32[]{:S(2)}, u32[]{:S(2)}) %collective-permute-start.6) | collective-permute-done | bytes 409632 | tf_op jit(solution)/shard_map/ppermute | solution.py:41
  353.6 20.1 %collective-permute-start.7 = (f32[256,800]{0,1:T(8,128)}, f32[256,800]{0,1:T(8,128)}, u32[]{:S(2)}, u32[]{:S(2)}) collective-permute-start(f32[256,800]{0,1:T(8,128)} %pad_maximum_fusion.3), channel_id=1, source_target_pairs={{0,2},{1,3},{2,0},{3,1},{4,6},{5,7},{6,4},{7,5},{8,10},{9,11},{10,... | collective-permute-start | bytes 2457608 | tf_op jit(solution)/shard_map/ppermute | solution.py:41
  375.9 6.2 %convolution_bitcast_fusion.1 = f32[192,2400]{1,0:T(8,128)} fusion(f32[512,2400]{0,1:T(8,128)} %fusion.7, f32[192,512]{1,0:T(8,128)S(1)} %copy-done.3), kind=kOutput, calls=%fused_computation.23 | convolution fusion | flops 1415577600 | bytes 7151616 | tf_op jit(solution)/shard_map/dot_general | solution.py:51
  382.1 5.7 %fusion.25 = f32[192,512]{1,0:T(8,128)} fusion(f32[192,2400]{1,0:T(8,128)} %bitcast.13, f32[2400,512]{1,0:T(8,128)} %bitcast.72), kind=kOutput, calls=%fused_computation.75 | convolution fusion | flops 1415577600 | bytes 7151616 | tf_op jit(solution)/shard_map/dot_general | solution.py:59
  395.0 4.4 all-to-all-start.3
  399.4 10.2 %collective-permute-done.7 = f32[256,800]{0,1:T(8,128)} collective-permute-done((f32[256,800]{0,1:T(8,128)}, f32[256,800]{0,1:T(8,128)}, u32[]{:S(2)}, u32[]{:S(2)}) %collective-permute-start.7) | collective-permute-done | bytes 819232 | tf_op jit(solution)/shard_map/ppermute | solution.py:41
  430.9 8.7 %all-to-all-done.4 = f32[8,8,2400]{2,1,0:T(8,128)S(1)} async-done(((f32[8,8,2400]{2,1,0:T(8,128)}), f32[8,8,2400]{2,1,0:T(8,128)S(1)}, u32[]{:S(2)}, u32[]{:S(2)}) %all-to-all-start.4) | async-done | bytes 614432 | tf_op jit(solution)/shard_map/all_to_all | solution.py:56
  456.3 6.6 %concatenate.48 = f32[192,6400]{1,0:T(8,128)} concatenate(f32[192,2400]{1,0:T(8,128)} %convolution_bitcast_fusion.3, f32[192,2400]{1,0:T(8,128)} %convolution_bitcast_fusion.1, f32[192,800]{1,0:T(8,128)} %convolution_bitcast_fusion.7, f32[192,800]{1,0:T(8,128)} %convolution_bitcast_fusion.5), dimensions={1} | concatenate | bytes 9830400 | tf_op jit(solution)/shard_map/concatenate | solution.py:61
  462.9 16.4 %all-to-all-done.5 = f32[32,128,64]{1,2,0:T(8,128)S(1)} async-done(((f32[32,128,64]{1,2,0:T(8,128)}), f32[32,128,64]{1,2,0:T(8,128)S(1)}, u32[]{:S(2)}, u32[]{:S(2)}) %all-to-all-start.5) | async-done | bytes 1048608 | tf_op jit(solution)/shard_map/all_to_all | solution.py:68
  (96 shorter events, 99.4 us)
Async XLA Ops:
  5.8 31.4 %collective-permute-start.2 = (f32[128,2400]{0,1:T(8,128)S(1)}, f32[128,2400]{0,1:T(8,128)S(1)}, u32[]{:S(2)}, u32[]{:S(2)}) collective-permute-start(f32[128,2400]{0,1:T(8,128)S(1)} %copy.72), channel_id=1, source_target_pairs={{0,3},{1,0},{2,1},{3,2},{4,7},{5,4},{6,5},{7,6},{8,11},{9,8},{10,9... | collective-permute-start | bytes 3686408 | tf_op jit(solution)/shard_map/ppermute | solution.py:41
  39.1 6.1 %copy-start.2 = (f32[192,512]{1,0:T(8,128)S(1)}, f32[192,512]{1,0:T(8,128)}, u32[]{:S(2)}) copy-start(f32[192,512]{1,0:T(8,128)} %param.9) | copy-start | bytes 1179652
  39.1 197.4 %collective-permute-start.3 = (f32[256,2400]{0,1:T(8,128)}, f32[256,2400]{0,1:T(8,128)}, u32[]{:S(2)}, u32[]{:S(2)}) collective-permute-start(f32[256,2400]{0,1:T(8,128)} %pad_maximum_fusion.1), channel_id=1, source_target_pairs={{0,2},{1,3},{2,0},{3,1},{4,6},{5,7},{6,4},{7,5},{8,10},{9,11},{10,... | collective-permute-start | bytes 7372808 | tf_op jit(solution)/shard_map/ppermute | solution.py:41
  42.3 78.7 %collective-permute-start = (f32[128,2400]{0,1:T(8,128)S(1)}, f32[128,2400]{0,1:T(8,128)}, u32[]{:S(2)}, u32[]{:S(2)}) collective-permute-start(f32[128,2400]{0,1:T(8,128)S(1)} %copy.71), channel_id=1, source_target_pairs={{0,3},{1,0},{2,1},{3,2},{4,7},{5,4},{6,5},{7,6},{8,11},{9,8},{10,9... | collective-permute-start | bytes 3686408 | tf_op jit(solution)/shard_map/ppermute | solution.py:41
  46.2 190.1 %all-to-all-start = ((f32[2,96,512]{2,0,1:T(2,128)}), f32[2,96,512]{2,0,1:T(2,128)S(1)}, u32[]{:S(2)}, u32[]{:S(2)}) async-start(f32[2,96,512]{2,0,1:T(2,128)} %copy.58), calls=%async_computation | async-start | bytes 786432 | tf_op jit(solution)/shard_map/all_to_all | solution.py:28
  123.8 165.3 %collective-permute-start.1 = (f32[256,2400]{0,1:T(8,128)}, f32[256,2400]{0,1:T(8,128)}, u32[]{:S(2)}, u32[]{:S(2)}) collective-permute-start(f32[256,2400]{0,1:T(8,128)} %pad_maximum_fusion), channel_id=1, source_target_pairs={{0,2},{1,3},{2,0},{3,1},{4,6},{5,7},{6,4},{7,5},{8,10},{9,11},{10,... | collective-permute-start | bytes 7372808 | tf_op jit(solution)/shard_map/ppermute | solution.py:41
  236.5 63.7 %copy-start.6 = (f32[4,2,24,512]{3,2,1,0:T(8,128)}, f32[4,2,24,512]{3,2,1,0:T(8,128)S(1)}, u32[]{:S(2)}) copy-start(f32[4,2,24,512]{3,2,1,0:T(8,128)S(1)} %copy.60) | copy-start | bytes 1179652
  264.5 29.8 %all-to-all-start.1 = ((f32[8,24,2400]{2,1,0:T(8,128)}), f32[8,24,2400]{2,1,0:T(8,128)}, u32[]{:S(2)}, u32[]{:S(2)}) async-start(f32[8,24,2400]{2,1,0:T(8,128)} %reshape.127), calls=%async_computation.1 | async-start | bytes 3735552 | tf_op jit(solution)/shard_map/all_to_all | solution.py:56
  272.0 52.1 %collective-permute-start.4 = (f32[128,800]{0,1:T(8,128)}, f32[128,800]{0,1:T(8,128)}, u32[]{:S(2)}, u32[]{:S(2)}) collective-permute-start(f32[128,800]{0,1:T(8,128)} %copy.73), channel_id=1, source_target_pairs={{0,3},{1,0},{2,1},{3,2},{4,7},{5,4},{6,5},{7,6},{8,11},{9,8},{10,9... | collective-permute-start | bytes 1228808 | tf_op jit(solution)/shard_map/ppermute | solution.py:41
  294.3 5.8 %copy-start = (f32[512,2400]{0,1:T(8,128)S(1)}, f32[512,2400]{0,1:T(8,128)}, u32[]{:S(2)}) copy-start(f32[512,2400]{0,1:T(8,128)} %fusion.7) | copy-start | bytes 14745604
  319.7 62.4 %all-to-all-start.2 = ((f32[8,24,2400]{2,1,0:T(8,128)}), f32[8,24,2400]{2,1,0:T(8,128)}, u32[]{:S(2)}, u32[]{:S(2)}) async-start(f32[8,24,2400]{2,1,0:T(8,128)} %reshape.131), calls=%async_computation.2 | async-start | bytes 3735552 | tf_op jit(solution)/shard_map/all_to_all | solution.py:56
  325.4 48.4 %collective-permute-start.5 = (f32[256,800]{0,1:T(8,128)S(1)}, f32[256,800]{0,1:T(8,128)}, u32[]{:S(2)}, u32[]{:S(2)}) collective-permute-start(f32[256,800]{0,1:T(8,128)S(1)} %pad_maximum_fusion.2), channel_id=1, source_target_pairs={{0,2},{1,3},{2,0},{3,1},{4,6},{5,7},{6,4},{7,5},{8,10},{9,11},{10,... | collective-permute-start | bytes 2457608 | tf_op jit(solution)/shard_map/ppermute | solution.py:41
  325.6 50.3 %copy-start.10 = (f32[128,800]{0,1:T(8,128)}, f32[128,800]{0,1:T(8,128)S(1)}, u32[]{:S(2)}) copy-start(f32[128,800]{0,1:T(8,128)S(1)} %copy.74) | copy-start | bytes 1228804
  325.6 50.3 %copy-start.3 = (f32[192,512]{1,0:T(8,128)S(1)}, f32[192,512]{1,0:T(8,128)}, u32[]{:S(2)}) copy-start(f32[192,512]{1,0:T(8,128)} %param.9) | copy-start | bytes 1179652
  325.7 26.9 %collective-permute-start.6 = (f32[128,800]{0,1:T(8,128)S(1)}, f32[128,800]{0,1:T(8,128)S(1)}, u32[]{:S(2)}, u32[]{:S(2)}) collective-permute-start(f32[128,800]{0,1:T(8,128)S(1)} %copy.74), channel_id=1, source_target_pairs={{0,3},{1,0},{2,1},{3,2},{4,7},{5,4},{6,5},{7,6},{8,11},{9,8},{10,9... | collective-permute-start | bytes 1228808 | tf_op jit(solution)/shard_map/ppermute | solution.py:41
  352.6 21.2 %copy-start.12 = (f32[128,800]{0,1:T(8,128)}, f32[128,800]{0,1:T(8,128)S(1)}, u32[]{:S(2)}) copy-start(f32[128,800]{0,1:T(8,128)S(1)} %collective-permute-done.6) | copy-start | bytes 1228804
  353.6 56.0 %collective-permute-start.7 = (f32[256,800]{0,1:T(8,128)}, f32[256,800]{0,1:T(8,128)}, u32[]{:S(2)}, u32[]{:S(2)}) collective-permute-start(f32[256,800]{0,1:T(8,128)} %pad_maximum_fusion.3), channel_id=1, source_target_pairs={{0,2},{1,3},{2,0},{3,1},{4,6},{5,7},{6,4},{7,5},{8,10},{9,11},{10,... | collective-permute-start | bytes 2457608 | tf_op jit(solution)/shard_map/ppermute | solution.py:41
  395.0 18.7 %all-to-all-start.3 = ((f32[8,8,2400]{2,1,0:T(8,128)}), f32[8,8,2400]{2,1,0:T(8,128)}, u32[]{:S(2)}, u32[]{:S(2)}) async-start(f32[8,8,2400]{2,1,0:T(8,128)} %reshape.134), calls=%async_computation.3 | async-start | bytes 1245184 | tf_op jit(solution)/shard_map/all_to_all | solution.py:56
  399.4 12.3 %copy-start.4 = (f32[192,512]{1,0:T(8,128)S(1)}, f32[192,512]{1,0:T(8,128)}, u32[]{:S(2)}) copy-start(f32[192,512]{1,0:T(8,128)} %param.9) | copy-start | bytes 1179652
  421.8 7.0 %copy-start.13 = (f32[192,512]{1,0:T(8,128)S(1)}, f32[192,512]{1,0:T(8,128)}, u32[]{:S(2)}) copy-start(f32[192,512]{1,0:T(8,128)} %fusion.24) | copy-start | bytes 1179652
  425.1 14.4 %all-to-all-start.4 = ((f32[8,8,2400]{2,1,0:T(8,128)}), f32[8,8,2400]{2,1,0:T(8,128)S(1)}, u32[]{:S(2)}, u32[]{:S(2)}) async-start(f32[8,8,2400]{2,1,0:T(8,128)} %reshape.140), calls=%async_computation.4 | async-start | bytes 1245184 | tf_op jit(solution)/shard_map/all_to_all | solution.py:56
  446.1 7.6 %copy-start.15 = (s32[96]{0:T(128)S(1)}, s32[96]{0:T(128)}, u32[]{:S(2)}) copy-start(s32[96]{0:T(128)} %param.12) | copy-start | bytes 1156
  446.1 8.3 %copy-start.5 = (f32[192,512]{1,0:T(8,128)S(1)}, f32[192,512]{1,0:T(8,128)}, u32[]{:S(2)}) copy-start(f32[192,512]{1,0:T(8,128)} %param.9) | copy-start | bytes 1179652
  449.3 30.0 %all-to-all-start.5 = ((f32[32,128,64]{1,2,0:T(8,128)}), f32[32,128,64]{1,2,0:T(8,128)S(1)}, u32[]{:S(2)}, u32[]{:S(2)}) async-start(f32[32,128,64]{1,2,0:T(8,128)} %bitcast.27), calls=%async_computation.5 | async-start | bytes 2097152 | tf_op jit(solution)/shard_map/all_to_all | solution.py:68
  (6 other events, 24.1 us)
